TPU v7x, 32 devices: a whole 2x2x4 slice. The times are simulated.
32 devices in a mesh: vis: 2 (over x), ctx: 8 (over z, y), tp: 2 (over core).
Axes of the slice: x: 2, y: 2, z: 4, core: 2. Of those that a mesh axis runs over, the one named last changes fastest.
Arguments:
- patch_rows: bfloat16 [1024, 1280], P('ctx'), may hold values from -6 to 6
- vit_gain: float32 [1280], replicated, may hold values from 0.25 to 1.75
- vit_bias: float32 [1280], replicated, may hold values from -3 to 3
- vit_qkv: bfloat16 [1280, 3, 16, 80], P(None, None, ('vis', 'tp')), as said below
- vit_out: bfloat16 [16, 80, 1280], P(('vis', 'tp')), may hold values from -0.15625 to 0.15625
- merge_gain: float32 [1280], replicated, may hold values from 0.25 to 1.75
- merge_bias: float32 [1280], replicated, may hold values from -3 to 3
- merge_weight: bfloat16 [5120, 4096], P('ctx', ('vis', 'tp')), may hold values from -0.078125 to 0.078125
- image_patches: int32 [8, 2], replicated, may hold values from 4 to 64, as said below
- window_ids: int32 [1024], P('ctx'), may hold values from 0 to 1023, as said below
- image_pos: int32 [256], replicated, may hold values from 0 to 1023, as said below
- slice_order: int32 [8], replicated, may hold values from 0 to 7, as said below
- doc_ids: int32 [1024], replicated, may hold values from 0 to 3, never falling along the last dimension, each value on 1 to 512 neighbouring positions
- text_rows: bfloat16 [1024, 4096], P('ctx', ('vis', 'tp')), may hold values from -6 to 6
- norm_gain: float32 [4096], replicated, may hold values from 0.25 to 1.75
- w_query: bfloat16 [4096, 8, 4, 128], P(None, 'vis', 'tp'), as said below
- w_keyval: bfloat16 [2, 4096, 8, 128], P('tp', None, 'vis'), as said below
Outputs:
- attention_out: bfloat16 [1024, 8, 512], P('ctx', 'vis', 'tp')
Inputs may be any that keep to these rules, and one draw needn't show every extreme that they name: `image_patches`: each is h * w for an image of h by w patches, h and w even and at most 32; the images of one ctx shard hold at most 128 patches together, exactly 128 on some shard. `window_ids`: equal ids mark one attention window: consecutive slots of one ctx shard, a multiple of 4 of them and at most 64, never in two images; slots after a shard's live patches form windows of 4. `slice_order`: a permutation; ctx shard c holds the sequence slices slice_order[c] and 15 - slice_order[c] of 64 positions, in that order, as its 128 rows. `image_pos`: distinct positions, one for every merged slot, live or not; the 32 slots of any one ctx shard put exactly 4 positions into the rows of each ctx shard. `doc_ids`: never falling along positions; each document holds 1 to 512 positions. `vit_qkv`: independent centred entries. `w_query`: independent centred entries. `w_keyval`: independent centred entries.
All inputs are finite; a program needn't handle non-finite values.
Results may differ from a plain program's by a relative error of at most 0.022.
The roundings to bfloat16 on the way count: a program that leaves them out, or rounds other values in their place, can miss the bound.
Values may be sent and summed in bfloat16 or wider, within the bound.
No kernel may reach another device: no remote copies, remote signals or barrier semaphores. Data moves between devices by JAX's collectives and lax.ppermute only.
A program may use at most 64 MiB of HBM per device.

v0:
```python
import math
import jax
import jax.numpy as jnp
from jax import lax
from jax.sharding import PartitionSpec as P

D = 4096
HD = 128
VD = 1280
VHD = 80
TOK = 128
PCAP = 128
ICAP = 32
norm_eps = 1e-06
rope_base = 1000000.0
big_negative = -1e30


def swapped(value, axis, stride):
    return lax.ppermute(value, axis, [(i, i ^ 1 << stride) for i in range(lax.axis_size(axis))])


def layer_norm(values, scale_vec, shift_vec):
    centre = jnp.mean(values, axis=-1, keepdims=True)
    offset = values - centre
    spread = jnp.mean(offset * offset, axis=-1, keepdims=True)
    return offset * lax.rsqrt(spread + norm_eps) * scale_vec + shift_vec


def rotate(values, positions):
    half_dim = values.shape[-1] // 2
    exponent = jnp.arange(half_dim, dtype=jnp.float32) * (-2.0 / values.shape[-1])
    frequency = jnp.power(jnp.float32(rope_base), exponent)
    angles = positions.astype(jnp.float32)[:, None] * frequency[None, :]
    shape_out = (values.shape[0],) + (1,) * (values.ndim - 2) + (half_dim,)
    cosine = jnp.cos(angles).reshape(shape_out)
    sine_part = jnp.sin(angles).reshape(shape_out)
    lead_half = values[..., :half_dim]
    tail_half = values[..., half_dim:]
    return jnp.concatenate(
        [lead_half * cosine - tail_half * sine_part, tail_half * cosine + lead_half * sine_part],
        axis=-1,
    )


def row_positions(row_ids, slice_order, tokens_dev):
    shards = slice_order.shape[0]
    device_of = row_ids // tokens_dev
    local_row = row_ids % tokens_dev
    half_tok = tokens_dev // 2
    matches = device_of[:, None] == jnp.arange(shards, dtype=jnp.int32)[None, :]
    first_slice = jnp.sum(jnp.where(matches, slice_order[None, :], 0), axis=1)
    slice_ids = jnp.where(local_row < half_tok, first_slice, 2 * shards - 1 - first_slice)
    return slice_ids * half_tok + local_row % half_tok


def place_of(positions, slice_order, tokens_dev):
    shards = slice_order.shape[0]
    half_tok = tokens_dev // 2
    slice_ids = positions // half_tok
    paired = jnp.minimum(slice_ids, 2 * shards - 1 - slice_ids)
    owner_hot = (paired[..., None] == slice_order).astype(jnp.int32)
    owner_dev = jnp.sum(owner_hot * jnp.arange(shards, dtype=jnp.int32), axis=-1)
    local_row = jnp.where(slice_ids < shards, 0, half_tok) + positions % half_tok
    return (owner_dev, local_row, owner_hot)


def local(
    patch_rows,
    vit_gain,
    vit_bias,
    vit_qkv,
    vit_out,
    merge_gain,
    merge_bias,
    merge_weight,
    image_patches,
    window_ids,
    image_pos,
    slice_order,
    doc_ids,
    text_rows,
    norm_gain,
    w_query,
    w_keyval,
):
    shards = lax.axis_size("ctx")
    ctx_index = lax.axis_index("ctx")
    tp_index = lax.axis_index("tp")
    vit_heads = vit_qkv.shape[2]
    slab_width = merge_weight.shape[1]
    normed = layer_norm(patch_rows.astype(jnp.float32), vit_gain, vit_bias).astype(jnp.bfloat16)
    projected = jnp.dot(
        normed, vit_qkv.reshape(VD, 3 * vit_heads * VHD), preferred_element_type=jnp.float32
    )
    projected = projected.astype(jnp.bfloat16).reshape(PCAP, 3, vit_heads, VHD)
    scores = jnp.einsum(
        "qhd,khd->hqk", projected[:, 0], projected[:, 1], preferred_element_type=jnp.float32
    ) / math.sqrt(VHD)
    allowed = window_ids[:, None] == window_ids[None, :]
    scores = jnp.where(allowed[None], scores, big_negative)
    powers = jnp.exp(scores - jnp.max(scores, axis=-1, keepdims=True))
    totals = jnp.sum(powers, axis=-1)
    blended = jnp.einsum(
        "hqk,khd->qhd",
        powers.astype(jnp.bfloat16),
        projected[:, 2],
        preferred_element_type=jnp.float32,
    )
    blended = (
        (blended / jnp.transpose(totals)[:, :, None])
        .astype(jnp.bfloat16)
        .reshape(PCAP, vit_heads * VHD)
    )
    out_flat = vit_out.reshape(vit_heads * VHD, VD)
    branch_part = jnp.dot(blended, out_flat, preferred_element_type=jnp.float32)
    branch_sum = lax.psum(branch_part, ("vis", "tp"))
    hidden = patch_rows.astype(jnp.float32) + branch_sum
    merged = layer_norm(hidden, merge_gain, merge_bias).astype(jnp.bfloat16).reshape(ICAP, 4 * VD)
    image_emb = jnp.dot(
        merged,
        lax.all_gather(merge_weight, "ctx", axis=0, tiled=True),
        preferred_element_type=jnp.float32,
    ).astype(jnp.bfloat16)
    send_each = ICAP // shards
    slot_ids = jnp.arange(ICAP, dtype=jnp.int32)
    shard_ids = jnp.arange(shards, dtype=jnp.int32)
    live_count = jnp.sum(image_patches, axis=1) // 4
    all_pos = image_pos.reshape(shards, ICAP)
    owner_dev, local_row, owner_hot = place_of(all_pos, slice_order, TOK)
    before = jnp.cumsum(owner_hot, axis=1) - owner_hot
    rank_in = jnp.sum(before * owner_hot, axis=-1)
    is_live = slot_ids[None, :] < live_count[:, None]
    own_hot = (shard_ids == ctx_index)[:, None]
    own_owner = jnp.sum(jnp.where(own_hot, owner_dev, 0), axis=0)
    own_rank = jnp.sum(jnp.where(own_hot, rank_in, 0), axis=0)
    own_live = jnp.any(own_hot & is_live, axis=0)
    target_slot = own_owner * send_each + own_rank
    picker = ((target_slot[None, :] == slot_ids[:, None]) & own_live[None, :]).astype(jnp.bfloat16)
    outgoing = jnp.dot(picker, image_emb, preferred_element_type=jnp.float32).astype(jnp.bfloat16)
    incoming = lax.all_to_all(
        outgoing.reshape(shards, send_each, slab_width),
        "ctx",
        split_axis=0,
        concat_axis=0,
        tiled=True,
    )
    mine_live = ((owner_dev == ctx_index) & is_live).reshape(-1)
    column_of = (shard_ids[:, None] * send_each + rank_in).reshape(-1)
    row_hot = (
        (local_row.reshape(-1)[None, :] == jnp.arange(TOK, dtype=jnp.int32)[:, None])
        & mine_live[None, :]
    ).astype(jnp.bfloat16)
    column_hot = (column_of[:, None] == slot_ids[None, :]).astype(jnp.bfloat16)
    placing = jnp.dot(row_hot, column_hot, preferred_element_type=jnp.float32)
    is_image = jnp.sum(placing, axis=1) > 0.5
    image_part = jnp.dot(
        placing.astype(jnp.bfloat16),
        incoming.reshape(ICAP, slab_width),
        preferred_element_type=jnp.float32,
    )
    embeds = jnp.where(is_image[:, None], image_part.astype(jnp.bfloat16), text_rows)
    full_rows = lax.all_gather(embeds, ("vis", "tp"), axis=1, tiled=True)
    widened = full_rows.astype(jnp.float32)
    normed_rows = (
        widened
        * lax.rsqrt(jnp.mean(widened * widened, axis=1, keepdims=True) + norm_eps)
        * norm_gain
    ).astype(jnp.bfloat16)
    own_positions = row_positions(
        ctx_index * TOK + jnp.arange(TOK, dtype=jnp.int32), slice_order, TOK
    )
    own_doc = jnp.take(doc_ids, own_positions)
    kv_heads = w_query.shape[1]
    groups = w_query.shape[2]
    queries = jnp.dot(
        normed_rows, w_query.reshape(D, kv_heads * groups * HD), preferred_element_type=jnp.float32
    ).reshape(TOK, kv_heads, groups, HD)
    queries = rotate(queries, own_positions).astype(jnp.bfloat16)
    projected_half = jnp.dot(
        normed_rows, w_keyval[0].reshape(D, kv_heads * HD), preferred_element_type=jnp.float32
    ).reshape(TOK, kv_heads, HD)
    own_half = jnp.where(
        tp_index == 0, rotate(projected_half, own_positions), projected_half
    ).astype(jnp.bfloat16)
    initial = (
        jnp.full((kv_heads, groups, TOK), big_negative, jnp.float32),
        jnp.zeros((kv_heads, groups, TOK), jnp.float32),
        jnp.zeros((kv_heads, groups, TOK, HD), jnp.float32),
    )
    gathered = lax.all_gather(own_half, "ctx", axis=0, tiled=True)
    partner_all = swapped(gathered, "tp", 0)
    keys_every = jnp.where(tp_index == 0, gathered, partner_all)
    values_every = jnp.where(tp_index == 0, partner_all, gathered)
    carry_state = initial
    key_count = keys_every.shape[0]
    block_rows = key_count if key_count <= 1024 else math.gcd(key_count, 1024)
    block_count = key_count // block_rows
    key_pos = row_positions(jnp.arange(key_count, dtype=jnp.int32), slice_order, TOK)
    key_doc = jnp.take(doc_ids, key_pos)
    stacked = (
        keys_every.reshape(block_count, block_rows, kv_heads, HD),
        values_every.reshape(block_count, block_rows, kv_heads, HD),
        key_pos.reshape(block_count, block_rows),
        key_doc.reshape(block_count, block_rows),
    )

    def key_block(state_now, inputs_now):
        keys_blk, values_blk, pos_blk, doc_blk = inputs_now
        best_old, total_old, accum_old = state_now
        allowed_now = (pos_blk[None, :] <= own_positions[:, None]) & (
            doc_blk[None, :] == own_doc[:, None]
        )
        scores_now = jnp.einsum(
            "qkgd,nkd->kgqn", queries, keys_blk, preferred_element_type=jnp.float32
        ) / math.sqrt(HD)
        scores_now = jnp.where(allowed_now[None, None], scores_now, big_negative)
        best_new = jnp.maximum(best_old, jnp.max(scores_now, axis=-1))
        factor = jnp.exp(best_old - best_new)
        powers_now = jnp.where(
            allowed_now[None, None], jnp.exp(scores_now - best_new[..., None]), 0.0
        )
        total_new = total_old * factor + jnp.sum(powers_now, axis=-1)
        accum_new = accum_old * factor[..., None] + jnp.einsum(
            "kgqn,nkd->kgqd",
            powers_now.astype(jnp.bfloat16),
            values_blk,
            preferred_element_type=jnp.float32,
        )
        return ((best_new, total_new, accum_new), None)

    carry_state, unused = lax.scan(key_block, carry_state, stacked)
    best_final, total_final, accum_final = carry_state
    result = accum_final / total_final[..., None]
    return (
        jnp.transpose(result, (2, 0, 1, 3)).reshape(TOK, kv_heads, groups * HD).astype(jnp.bfloat16)
    )


def solution(mesh):
    placed = (
        P("ctx", None),
        P(),
        P(),
        P(None, None, ("vis", "tp"), None),
        P(("vis", "tp"), None, None),
        P(),
        P(),
        P("ctx", ("vis", "tp")),
        P(),
        P("ctx"),
        P(),
        P(),
        P(),
        P("ctx", ("vis", "tp")),
        P(),
        P(None, "vis", "tp", None),
        P("tp", None, "vis", None),
    )
    return jax.shard_map(
        local, mesh=mesh, in_specs=placed, out_specs=P("ctx", "vis", "tp"), check_vma=False
    )
```

profile of v0, /device:TPU:1, one launch (start us, length us, event | category | flops | bytes accessed | tf_op | source)
XLA Modules:
  0.0 267.5 jit_solution(11337003461193074470)
XLA Ops:
  7.4 1.2 convert_reduce_fusion
  8.7 1.3 fusion.43
  9.9 0.8 broadcast_compare_fusion
  10.8 1.9 convolution_convert_fusion.1
  13.0 2.5 convolution_bitcast_fusion
  17.1 0.7 fusion.110
  18.6 32.0 %all-reduce.2.cloned.1.call-done = f32[128,1280]{1,0:T(8,128)} async-done(((f32[128,1280]{1,0:T(8,128)}), f32[128,1280]{1,0:T(8,128)}) %all-reduce.2.cloned.1.call-update) | async-done | bytes 655376 | tf_op jit(solution)/shard_map/psum | solution.py:117
  50.5 1.2 fusion.58
  51.8 1.3 multiply_reduce_fusion
  53.1 1.3 add_convert_fusion
  54.6 114.9 %all-gather.4.cloned.1.call-done = bf16[5120,1024]{1,0:T(8,128)(2,1)} async-done(((bf16[640,1024]{1,0:T(8,128)(2,1)}), bf16[5120,1024]{1,0:T(8,128)(2,1)}) %all-gather.4.cloned.1.call-update) | async-done | bytes 10485776 | tf_op jit(solution)/shard_map/all_gather | solution.py:122
  169.5 6.1 %convolution_convert_fusion.2 = bf16[32,1024]{1,0:T(8,128)(2,1)S(1)} fusion(bf16[32,5120]{1,0:T(8,128)(2,1)S(1)} %reshape.660, bf16[5120,1024]{1,0:T(8,128)(2,1)} %all-gather.4.cloned.1.call-done, s32[32]{0:T(128)S(1)} %multiply_add_fusion.1, pred[32]{0:T(512)(128)(4,1)S(1)} %get-tuple-element.54), kind=kOutput, calls=%fused_computation.28 | convolution fusion | flops 337709056 | bytes 10879136 | tf_op jit(solution)/shard_map/dot_general | solution.py:140
  176.3 3.4 %all-to-all-start = ((bf16[8,4,1024]{2,1,0:T(4,128)(2,1)}), bf16[8,4,1024]{2,1,0:T(4,128)(2,1)S(1)}, u32[]{:S(2)}, u32[]{:S(2)}) async-start(bf16[8,4,1024]{2,1,0:T(4,128)(2,1)} %reshape.661), calls=%async_computation | async-start | bytes 131072 | tf_op jit(solution)/shard_map/all_to_all | solution.py:141
  179.7 5.6 %all-to-all-done = bf16[8,4,1024]{2,1,0:T(4,128)(2,1)S(1)} async-done(((bf16[8,4,1024]{2,1,0:T(4,128)(2,1)}), bf16[8,4,1024]{2,1,0:T(4,128)(2,1)S(1)}, u32[]{:S(2)}, u32[]{:S(2)}) %all-to-all-start) | async-done | bytes 65568 | tf_op jit(solution)/shard_map/all_to_all | solution.py:141
  185.4 1.0 fusion.16
  186.7 1.0 gather_fusion.1
  188.2 4.9 %copy.79 = bf16[512,8,4,128]{3,1,2,0:T(8,128)(2,1)} copy(bf16[512,8,4,128]{3,2,1,0:T(4,128)(2,1)} %bitcast.116) | data formatting | bytes 8388608
  193.1 6.5 %copy.63 = bf16[512,4096]{1,0:T(8,128)(2,1)} copy(bf16[512,4096]{0,1:T(8,128)(2,1)} %bitcast.114) | data formatting | bytes 8388608 | tf_op jit(solution)/shard_map/dot_general | solution.py:180
  199.8 3.1 %all-gather.6.cloned.1.call-done = bf16[128,4096]{1,0:T(8,128)(2,1)} async-done(((bf16[128,1024]{1,0:T(8,128)(2,1)}), bf16[128,4096]{1,0:T(8,128)(2,1)}) %all-gather.6.cloned.1.call-update) | async-done | bytes 1048592 | tf_op jit(solution)/shard_map/all_gather | solution.py:163
  203.0 1.5 fusion.3
  204.5 3.8 %fusion.25 = f32[128,4,128]{0,2,1:T(8,128)S(1)} fusion(bf16[4,128,4096]{2,1,0:T(8,128)(2,1)} %bitcast.117, bf16[128,4096]{1,0:T(8,128)(2,1)} %all-gather.6.cloned.1.call-done, f32[4096]{0:T(1024)S(1)} %copy-done.14, f32[128]{0:T(128)S(1)} %add_rsqrt_fusion), kind=kOutput, calls=%fused_computation.35 | convolution fusion | flops 538968064 | bytes 5521920 | tf_op jit(solution)/shard_map/dot_general | solution.py:180
  209.3 4.5 %gather_fusion = s32[1024]{0:T(1024)S(1)} fusion(s32[1024]{0:T(1024)S(1)} %copy-done.1, s32[1024]{0:T(1024)S(1)} %broadcast_clamp_fusion), kind=kCustom, calls=%fused_computation | custom fusion | bytes 12288 | tf_op jit(solution)/shard_map/jit(_take)/gather | solution.py:200
  213.8 14.4 %reshape.663 = bf16[4096,1024]{1,0:T(8,128)(2,1)} reshape(bf16[4096,4,2,128]{3,2,1,0:T(2,128)(2,1)} %param.32) | data formatting | bytes 16777216 | tf_op jit(solution)/shard_map/reshape | solution.py:177
  228.2 11.4 %copy.64 = bf16[1024,4096]{1,0:T(8,128)(2,1)} copy(bf16[1024,4096]{0,1:T(8,128)(2,1)} %bitcast.113) | data formatting | bytes 16777216 | tf_op jit(solution)/shard_map/dot_general | solution.py:176
  239.5 6.1 %all-gather.8.cloned.1.call-done = bf16[1024,4,128]{0,2,1:T(8,128)(2,1)} async-done(((bf16[128,4,128]{0,2,1:T(8,128)(2,1)}), bf16[1024,4,128]{0,2,1:T(8,128)(2,1)}) %all-gather.8.cloned.1.call-update) | async-done | bytes 1048592 | tf_op jit(solution)/shard_map/all_gather | solution.py:191
  245.6 3.2 %collective-permute-start = (bf16[1024,4,128]{0,2,1:T(8,128)(2,1)}, bf16[1024,4,128]{0,2,1:T(8,128)(2,1)S(1)}, u32[]{:S(2)}, u32[]{:S(2)}) collective-permute-start(bf16[1024,4,128]{0,2,1:T(8,128)(2,1)} %all-gather.8.cloned.1.call-done), channel_id=1, source_target_pairs={{0,1},{1,0},{2,3},{3,2},{4,5},{5,4},{6,7},{7,6},{8,9},{9,8},{10,11... | collective-permute-start | bytes 3145736 | tf_op jit(solution)/shard_map/ppermute | solution.py:20
  248.8 0.9 compare_and_fusion
  249.8 5.9 %fusion.23 = f32[128,4,2,128]{0,3,2,1:T(8,128)S(1)} fusion(bf16[4,2,128,4096]{3,2,1,0:T(8,128)(2,1)} %bitcast.115, bf16[128,4096]{1,0:T(8,128)(2,1)S(1)} %copy-done.3, f32[4096]{0:T(1024)} %param.31, f32[128]{0:T(128)} %copy-done.15), kind=kOutput, calls=%fused_computation.33 | convolution fusion | flops 1075838976 | bytes 9978368 | tf_op jit(solution)/shard_map/dot_general | solution.py:176
  255.8 1.0 fusion
  256.8 1.0 fusion.1
  257.9 1.3 fusion.36
  259.2 0.9 copy.68
  (87 shorter events, 5.7 us)
Async XLA Ops:
  7.4 3.4 %copy-start = (bf16[1280,3,4,80]{0,3,2,1:T(8,128)(2,1)S(1)}, bf16[1280,3,4,80]{0,3,2,1:T(8,128)(2,1)}, u32[]{:S(2)}) copy-start(bf16[1280,3,4,80]{0,3,2,1:T(8,128)(2,1)} %param.20) | copy-start | bytes 7372804
  7.4 8.8 %copy-start.10 = (s32[256]{0:T(256)S(1)}, s32[256]{0:T(256)}, u32[]{:S(2)}) copy-start(s32[256]{0:T(256)} %param.27) | copy-start | bytes 3076
  7.4 9.0 %copy-start.9 = (s32[8]{0:T(128)S(1)}, s32[8]{0:T(128)}, u32[]{:S(2)}) copy-start(s32[8]{0:T(128)} %param.28) | copy-start | bytes 100
  7.4 43.2 %all-reduce.2.cloned.1.call-start = ((), (), s32[]{:S(2)}) async-start(), calls=%async_computation.1 | async-start | bytes 1310720 | tf_op jit(solution)/shard_map/psum | solution.py:117
  8.6 9.4 %copy-start.12 = (s32[8,2]{0,1:T(2,128)S(1)}, s32[8,2]{0,1:T(2,128)}, u32[]{:S(2)}) copy-start(s32[8,2]{0,1:T(2,128)} %param.25) | copy-start | bytes 196
  8.6 41.9 %copy-start.2 = (bf16[128,1280]{1,0:T(8,128)(2,1)S(1)}, bf16[128,1280]{1,0:T(8,128)(2,1)}, u32[]{:S(2)}) copy-start(bf16[128,1280]{1,0:T(8,128)(2,1)} %param.17) | copy-start | bytes 983044
  12.7 40.5 %copy-start.7 = (f32[1280]{0:T(1024)S(1)}, f32[1280]{0:T(1024)}, u32[]{:S(2)}) copy-start(f32[1280]{0:T(1024)} %param.23) | copy-start | bytes 15364
  12.7 40.5 %copy-start.8 = (f32[1280]{0:T(1024)S(1)}, f32[1280]{0:T(1024)}, u32[]{:S(2)}) copy-start(f32[1280]{0:T(1024)} %param.22) | copy-start | bytes 15364
  15.6 154.0 %all-gather.4.cloned.1.call-start = ((), (), s32[]{:S(2)}) async-start(), calls=%async_computation.2 | async-start | bytes 11796480 | tf_op jit(solution)/shard_map/all_gather | solution.py:122
  169.5 15.8 %copy-start.6 = (bf16[128,1024]{1,0:T(8,128)(2,1)S(1)}, bf16[128,1024]{1,0:T(8,128)(2,1)}, u32[]{:S(2)}) copy-start(bf16[128,1024]{1,0:T(8,128)(2,1)} %param.30) | copy-start | bytes 786436
  169.5 17.2 %copy-start.1 = (s32[1024]{0:T(1024)S(1)}, s32[1024]{0:T(1024)}, u32[]{:S(2)}) copy-start(s32[1024]{0:T(1024)} %param.29) | copy-start | bytes 12292
  176.3 9.1 %all-to-all-start = ((bf16[8,4,1024]{2,1,0:T(4,128)(2,1)}), bf16[8,4,1024]{2,1,0:T(4,128)(2,1)S(1)}, u32[]{:S(2)}, u32[]{:S(2)}) async-start(bf16[8,4,1024]{2,1,0:T(4,128)(2,1)} %reshape.661), calls=%async_computation | async-start | bytes 131072 | tf_op jit(solution)/shard_map/all_to_all | solution.py:141
  179.6 23.3 %all-gather.6.cloned.1.call-start = ((), (), s32[]{:S(2)}) async-start(), calls=%async_computation.3 | async-start | bytes 1310720 | tf_op jit(solution)/shard_map/all_gather | solution.py:163
  186.3 59.3 %all-gather.8.cloned.1.call-start = ((), (), s32[]{:S(2)}) async-start(), calls=%async_computation.4 | async-start | bytes 1179648 | tf_op jit(solution)/shard_map/all_gather | solution.py:191
  188.2 4.9 %copy-start.11 = (s32[128]{0:T(128)}, s32[128]{0:T(128)S(1)}, u32[]{:S(2)}) copy-start(s32[128]{0:T(128)S(1)} %get-tuple-element.30) | copy-start | bytes 1540
  193.1 11.4 %copy-start.14 = (f32[4096]{0:T(1024)S(1)}, f32[4096]{0:T(1024)}, u32[]{:S(2)}) copy-start(f32[4096]{0:T(1024)} %param.31) | copy-start | bytes 49156
  199.8 8.5 %copy-start.4 = (f32[128,64]{0,1:T(8,128)}, f32[128,64]{0,1:T(8,128)S(1)}, u32[]{:S(2)}) copy-start(f32[128,64]{0,1:T(8,128)S(1)} %get-tuple-element.52) | copy-start | bytes 98308
  204.5 4.6 %copy-start.15 = (f32[128]{0:T(128)}, f32[128]{0:T(128)S(1)}, u32[]{:S(2)}) copy-start(f32[128]{0:T(128)S(1)} %add_rsqrt_fusion) | copy-start | bytes 1540
  228.2 21.6 %copy-start.3 = (bf16[128,4096]{1,0:T(8,128)(2,1)S(1)}, bf16[128,4096]{1,0:T(8,128)(2,1)}, u32[]{:S(2)}) copy-start(bf16[128,4096]{1,0:T(8,128)(2,1)} %all-gather.6.cloned.1.call-done) | copy-start | bytes 3145732
  245.6 10.1 %collective-permute-start = (bf16[1024,4,128]{0,2,1:T(8,128)(2,1)}, bf16[1024,4,128]{0,2,1:T(8,128)(2,1)S(1)}, u32[]{:S(2)}, u32[]{:S(2)}) collective-permute-start(bf16[1024,4,128]{0,2,1:T(8,128)(2,1)} %all-gather.8.cloned.1.call-done), channel_id=1, source_target_pairs={{0,1},{1,0},{2,3},{3,2},{4,5},{5,4},{6,7},{7,6},{8,9},{9,8},{10,11... | collective-permute-start | bytes 3145736 | tf_op jit(solution)/shard_map/ppermute | solution.py:20
  249.8 5.9 %copy-start.5 = (f32[128,64]{0,1:T(8,128)S(1)}, f32[128,64]{0,1:T(8,128)}, u32[]{:S(2)}) copy-start(f32[128,64]{0,1:T(8,128)} %copy-done.4) | copy-start | bytes 98308
  249.8 6.0 %copy-start.13 = (bf16[1024,4,128]{0,2,1:T(8,128)(2,1)S(1)}, bf16[1024,4,128]{0,2,1:T(8,128)(2,1)}, u32[]{:S(2)}) copy-start(bf16[1024,4,128]{0,2,1:T(8,128)(2,1)} %all-gather.8.cloned.1.call-done) | copy-start | bytes 3145732
Sparse Core Ops, SparseCore 0:
  15.7 34.8 all-reduce.1
  186.5 16.4 all-gather.5
Sparse Core Ops, SparseCore 1:
  18.2 151.2 all-gather.3
  209.2 36.4 all-gather.7
where the time goes:
time: 269 us; the launch traced here: 267 us
  waiting for transfers between devices  162 us (60%)
  local copies, waits for them, and re-layouts  44.9 us (17%)
  matrix products  24 us (9%)
  between operations  15.2 us (6%)
  other arithmetic  14.2 us (5%)
  starting transfers between devices  6.82 us (3%)
    all_gather x1, waiting for transfers between devices, local(): lax.all_gather(merge_weight, 'ctx', axis=0, tiled=True)  115 us
    psum x1, waiting for transfers between devices, local(): branch_sum = lax.psum(branch_part, ('vis', 'tp'))  32 us
    reshape x1, local copies, waits for them, and re-layouts, local(): w_query.reshape(D, kv_heads * groups * HD)  14.4 us
    dot_general x1, local copies, waits for them, and re-layouts, local(): jnp.dot(normed_rows, w_query.reshape(D, kv_heads * groups * HD), preferre...  11.4 us
    dot_general x1, local copies, waits for them, and re-layouts, local(): jnp.dot(normed_rows, w_keyval[0].reshape(D, kv_heads * HD), preferred_ele...  6.52 us
    all_gather x1, waiting for transfers between devices, local(): gathered = lax.all_gather(own_half, 'ctx', axis=0, tiled=True)  6.11 us
    dot_general x1, matrix products, local(): jnp.dot(picker, image_emb, preferred_element_type=jnp.float32)  6.07 us
    dot_general x1, matrix products, local(): jnp.dot(normed_rows, w_query.reshape(D, kv_heads * groups * HD), preferre...  5.89 us
  transfers between devices with their start and end apart: 6, of which 5 were waited for; matrix products, arithmetic and copies ran while one was open for 21% of the time, Pallas kernels for 0%

commit v1 on v0

--- a/solution.py
+++ b/solution.py
@@ -14,6 +14,25 @@
 norm_eps = 1e-06
 rope_base = 1000000.0
 big_negative = -1e30
+
+
+def records_search(array_here):
+    moved = jax.lax.axis_size("ctx")
+    t_next = jax.lax.axis_index("ctx")
+    mixed_arr, top, current_arr = (moved, t_next, array_here.shape[0])
+    local_out, n_now = (array_here, 1)
+    while n_now < mixed_arr:
+        local_out = jnp.concatenate(
+            [
+                local_out,
+                jax.lax.ppermute(
+                    local_out, "ctx", [(s, (s - n_now) % mixed_arr) for s in range(mixed_arr)]
+                ),
+            ],
+            0,
+        )
+        n_now = 2 * n_now
+    return jnp.roll(local_out, top * current_arr, 0)
 
 
 def swapped(value, axis, stride):
@@ -118,9 +137,7 @@
     hidden = patch_rows.astype(jnp.float32) + branch_sum
     merged = layer_norm(hidden, merge_gain, merge_bias).astype(jnp.bfloat16).reshape(ICAP, 4 * VD)
     image_emb = jnp.dot(
-        merged,
-        lax.all_gather(merge_weight, "ctx", axis=0, tiled=True),
-        preferred_element_type=jnp.float32,
+        merged, records_search(merge_weight), preferred_element_type=jnp.float32
     ).astype(jnp.bfloat16)
     send_each = ICAP // shards
     slot_ids = jnp.arange(ICAP, dtype=jnp.int32)

time: 269 us -> 454 us (1.69)
  waiting for transfers between devices: 162 us -> 317 us
  local copies, waits for them, and re-layouts: 44.9 us -> 66.7 us
  starting transfers between devices: 6.82 us -> 16.6 us
    ppermute x0 -> x3, waiting for transfers between devices: none -> 260 us  [records_search(): jax.lax.ppermute(local_out, 'ctx', [(s, (s - n_now) % mixed_arr) for s in...]
    all_gather x1 -> x0, waiting for transfers between devices: 115 us -> none  [local(): lax.all_gather(merge_weight, 'ctx', axis=0, tiled=True)]
    unnamed x33 -> x54, local copies, waits for them, and re-layouts: 4.95 us -> 21.6 us
    all_gather x1, waiting for transfers between devices: 3.11 us -> 17 us  [local(): full_rows = lax.all_gather(embeds, ('vis', 'tp'), axis=1, tiled=True)]
    ppermute x0 -> x3, starting transfers between devices: none -> 6.53 us  [records_search(): jax.lax.ppermute(local_out, 'ctx', [(s, (s - n_now) % mixed_arr) for s in...]
    all_to_all x1, waiting for transfers between devices: 5.63 us -> 0.01 us  [local(): lax.all_to_all(outgoing.reshape(shards, send_each, slab_width), 'ctx', sp...]
    concatenate x0 -> x2, other arithmetic: none -> 5.31 us  [records_search(): jnp.concatenate([local_out, jax.lax.ppermute(local_out, 'ctx', [(s, (s -...]
    concatenate x0 -> x1, local copies, waits for them, and re-layouts: none -> 5.3 us  [records_search(): return jnp.roll(local_out, top * current_arr, 0)]
  transfers between devices with their start and end apart: 6 -> 8, of which waited for: 5 -> 6; matrix products, arithmetic and copies ran while one was open for 21% -> 15% of each run, Pallas kernels for 0% -> 0%
where the time goes in v1:
time: 454 us; the launch traced here: 453 us
  waiting for transfers between devices  317 us (70%)
  local copies, waits for them, and re-layouts  66.7 us (15%)
  matrix products  23.9 us (5%)
  starting transfers between devices  16.6 us (4%)
  other arithmetic  15.5 us (3%)
  between operations  13.5 us (3%)
    ppermute x3, waiting for transfers between devices, records_search(): jax.lax.ppermute(local_out, 'ctx', [(s, (s - n_now) % mixed_arr) for s in...  260 us
    psum x1, waiting for transfers between devices, local(): branch_sum = lax.psum(branch_part, ('vis', 'tp'))  33.7 us
    unnamed x54, local copies, waits for them, and re-layouts  21.6 us
    all_gather x1, waiting for transfers between devices, local(): full_rows = lax.all_gather(embeds, ('vis', 'tp'), axis=1, tiled=True)  17 us
    reshape x1, local copies, waits for them, and re-layouts, local(): w_query.reshape(D, kv_heads * groups * HD)  14.4 us
    dot_general x1, local copies, waits for them, and re-layouts, local(): jnp.dot(normed_rows, w_query.reshape(D, kv_heads * groups * HD), preferre...  11.3 us
  transfers between devices with their start and end apart: 8, of which 6 were waited for; matrix products, arithmetic and copies ran while one was open for 15% of the time, Pallas kernels for 0%

profile of v1, /device:TPU:1, one launch (start us, length us, event | category | flops | bytes accessed | tf_op | source)
XLA Modules:
  0.0 453.1 jit_solution(987767087560467640)
XLA Ops:
  6.5 5.1 %collective-permute-start = (bf16[640,1024]{1,0:T(8,128)(2,1)}, bf16[640,1024]{1,0:T(8,128)(2,1)S(1)}, u32[]{:S(2)}, u32[]{:S(2)}) collective-permute-start(bf16[640,1024]{1,0:T(8,128)(2,1)} %param.24), channel_id=1, source_target_pairs={{0,14},{2,0},{4,2},{6,4},{8,6},{10,8},{12,10},{14,12},{1,15},{3,1}... | collective-permute-start | bytes 3932168 | tf_op jit(solution)/shard_map/ppermute | solution.py:28
  11.7 27.8 %collective-permute-done = bf16[640,1024]{1,0:T(8,128)(2,1)S(1)} collective-permute-done((bf16[640,1024]{1,0:T(8,128)(2,1)}, bf16[640,1024]{1,0:T(8,128)(2,1)S(1)}, u32[]{:S(2)}, u32[]{:S(2)}) %collective-permute-start) | collective-permute-done | bytes 1310752 | tf_op jit(solution)/shard_map/ppermute | solution.py:28
  39.5 2.1 pad_maximum_fusion.1
  41.6 1.2 collective-permute-start.1
  43.2 55.3 %collective-permute-done.1 = bf16[1280,1024]{1,0:T(8,128)(2,1)S(1)} collective-permute-done((bf16[1280,1024]{1,0:T(8,128)(2,1)S(1)}, bf16[1280,1024]{1,0:T(8,128)(2,1)S(1)}, u32[]{:S(2)}, u32[]{:S(2)}) %collective-permute-start.1) | collective-permute-done | bytes 2621472 | tf_op jit(solution)/shard_map/ppermute | solution.py:28
  98.6 3.2 pad_maximum_fusion
  103.3 2.5 convolution_bitcast_fusion
  108.1 2.5 constant_dynamic-update-slice_fusion.7
  110.9 33.7 %all-reduce.2.cloned.1.call-done = f32[128,1280]{1,0:T(8,128)} async-done(((f32[128,1280]{1,0:T(8,128)}), f32[128,1280]{1,0:T(8,128)}) %all-reduce.2.cloned.1.call-update) | async-done | bytes 655376 | tf_op jit(solution)/shard_map/psum | solution.py:136
  144.6 1.2 fusion.69
  145.8 1.3 multiply_reduce_fusion
  147.2 1.3 add_convert_fusion
  149.8 3.5 constant_dynamic-update-slice_fusion.5
  153.4 176.4 %collective-permute-done.2 = bf16[2560,1024]{1,0:T(8,128)(2,1)} collective-permute-done((bf16[2560,1024]{1,0:T(8,128)(2,1)}, bf16[2560,1024]{1,0:T(8,128)(2,1)}, u32[]{:S(2)}, u32[]{:S(2)}) %collective-permute-start.2) | collective-permute-done | bytes 5242912 | tf_op jit(solution)/shard_map/ppermute | solution.py:28
  329.8 5.4 %constant_dynamic-update-slice_fusion.4 = bf16[10240,1024]{1,0:T(8,128)(2,1)} fusion(bf16[10240,1024]{1,0:T(8,128)(2,1)} %constant_dynamic-update-slice_fusion.5, bf16[2560,1024]{1,0:T(8,128)(2,1)} %collective-permute-done.2), kind=kLoop, calls=%fused_computation.106 | loop fusion | bytes 10485760
  336.4 1.2 constant_dynamic-update-slice_fusion.2
  337.6 1.7 constant_dynamic-update-slice_fusion.1
  339.3 5.3 %constant_dynamic-update-slice_fusion = bf16[10240,1024]{1,0:T(8,128)(2,1)} fusion(bf16[10240,1024]{1,0:T(8,128)(2,1)} %constant_dynamic-update-slice_fusion.1, bf16[2560,1024]{1,0:T(8,128)(2,1)} %collective-permute-done.2), kind=kLoop, calls=%fused_computation.102 | loop fusion | bytes 10485760 | tf_op jit(solution)/shard_map/jit(_roll_dynamic)/concatenate | solution.py:35
  344.6 6.9 %fusion.28 = bf16[32,1024]{1,0:T(8,128)(2,1)S(1)} fusion(bf16[32,5120]{1,0:T(8,128)(2,1)S(1)} %reshape.660, bf16[10240,1024]{1,0:T(8,128)(2,1)} %constant_dynamic-update-slice_fusion, s32[]{:T(128)S(6)} %select_n.320, s32[32]{0:T(128)S(1)} %multiply_add_fusion.1, pred[32]{0:T(512)(128)(4,1)S(1)} %get-tuple-element.54), kind=kOutput, calls=%fused_computation.34 | convolution fusion | flops 337709056 | bytes 10879140 | tf_op jit(solution)/shard_map/dot_general | solution.py:157
  352.2 6.7 %all-to-all-start = ((bf16[8,4,1024]{2,1,0:T(4,128)(2,1)}), bf16[8,4,1024]{2,1,0:T(4,128)(2,1)S(1)}, u32[]{:S(2)}, u32[]{:S(2)}) async-start(bf16[8,4,1024]{2,1,0:T(4,128)(2,1)} %reshape.661), calls=%async_computation | async-start | bytes 131072 | tf_op jit(solution)/shard_map/all_to_all | solution.py:158
  358.9 4.9 %copy.79 = bf16[512,8,4,128]{3,1,2,0:T(8,128)(2,1)} copy(bf16[512,8,4,128]{3,2,1,0:T(4,128)(2,1)} %bitcast.115) | data formatting | bytes 8388608
  363.8 6.5 %copy.63 = bf16[512,4096]{1,0:T(8,128)(2,1)} copy(bf16[512,4096]{0,1:T(8,128)(2,1)} %bitcast.113) | data formatting | bytes 8388608 | tf_op jit(solution)/shard_map/dot_general | solution.py:197
  373.0 17.0 %all-gather.3.cloned.1.call-done = bf16[128,4096]{1,0:T(8,128)(2,1)} async-done(((bf16[128,1024]{1,0:T(8,128)(2,1)}), bf16[128,4096]{1,0:T(8,128)(2,1)}) %all-gather.3.cloned.1.call-update) | async-done | bytes 1048592 | tf_op jit(solution)/shard_map/all_gather | solution.py:180
  390.0 1.5 fusion.5
  391.5 3.8 fusion.36
  396.1 14.4 %reshape.663 = bf16[4096,1024]{1,0:T(8,128)(2,1)} reshape(bf16[4096,4,2,128]{3,2,1,0:T(2,128)(2,1)} %param.32) | data formatting | bytes 16777216 | tf_op jit(solution)/shard_map/reshape | solution.py:194
  410.5 11.3 %copy.64 = bf16[1024,4096]{1,0:T(8,128)(2,1)} copy(bf16[1024,4096]{0,1:T(8,128)(2,1)} %bitcast.112) | data formatting | bytes 16777216 | tf_op jit(solution)/shard_map/dot_general | solution.py:193
  421.7 4.5 gather_fusion
  426.3 6.5 %all-gather.5.cloned.1.call-done = bf16[1024,4,128]{0,2,1:T(8,128)(2,1)} async-done(((bf16[128,4,128]{0,2,1:T(8,128)(2,1)}), bf16[1024,4,128]{0,2,1:T(8,128)(2,1)}) %all-gather.5.cloned.1.call-update) | async-done | bytes 1048592 | tf_op jit(solution)/shard_map/all_gather | solution.py:208
  432.8 3.2 collective-permute-start.3
  436.3 5.9 %fusion.34 = f32[128,4,2,128]{0,3,2,1:T(8,128)S(1)} fusion(bf16[4,2,128,4096]{3,2,1,0:T(8,128)(2,1)} %bitcast.114, bf16[128,4096]{1,0:T(8,128)(2,1)S(1)} %copy-done.11, f32[4096]{0:T(1024)S(1)} %copy-done.20, f32[128]{0:T(128)S(1)} %add_rsqrt_fusion), kind=kOutput, calls=%fused_computation.38 | convolution fusion | flops 1075838976 | bytes 9978368 | tf_op jit(solution)/shard_map/dot_general | solution.py:193
  444.4 1.3 fusion.47
  (113 shorter events, 14.4 us)
Async XLA Ops:
  6.5 95.5 %copy-start = (bf16[1280,3,4,80]{0,3,2,1:T(8,128)(2,1)S(1)}, bf16[1280,3,4,80]{0,3,2,1:T(8,128)(2,1)}, u32[]{:S(2)}) copy-start(bf16[1280,3,4,80]{0,3,2,1:T(8,128)(2,1)} %param.20) | copy-start | bytes 7372804
  6.5 36.3 %copy-start.10 = (bf16[128,1280]{1,0:T(8,128)(2,1)S(1)}, bf16[128,1280]{1,0:T(8,128)(2,1)}, u32[]{:S(2)}) copy-start(bf16[128,1280]{1,0:T(8,128)(2,1)} %param.17) | copy-start | bytes 983044
  6.5 138.1 %all-reduce.2.cloned.1.call-start = ((), (), s32[]{:S(2)}) async-start(), calls=%async_computation.1 | async-start | bytes 1310720 | tf_op jit(solution)/shard_map/psum | solution.py:136
  6.5 92.0 %copy-start.5 = (bf16[640,1024]{1,0:T(8,128)(2,1)S(1)}, bf16[640,1024]{1,0:T(8,128)(2,1)}, u32[]{:S(2)}) copy-start(bf16[640,1024]{1,0:T(8,128)(2,1)} %param.24) | copy-start | bytes 3932164
  6.5 32.9 %collective-permute-start = (bf16[640,1024]{1,0:T(8,128)(2,1)}, bf16[640,1024]{1,0:T(8,128)(2,1)S(1)}, u32[]{:S(2)}, u32[]{:S(2)}) collective-permute-start(bf16[640,1024]{1,0:T(8,128)(2,1)} %param.24), channel_id=1, source_target_pairs={{0,14},{2,0},{4,2},{6,4},{8,6},{10,8},{12,10},{14,12},{1,15},{3,1}... | collective-permute-start | bytes 3932168 | tf_op jit(solution)/shard_map/ppermute | solution.py:28
  39.5 62.3 %copy-start.7 = (bf16[640,1024]{1,0:T(8,128)(2,1)}, bf16[640,1024]{1,0:T(8,128)(2,1)S(1)}, u32[]{:S(2)}) copy-start(bf16[640,1024]{1,0:T(8,128)(2,1)S(1)} %collective-permute-done) | copy-start | bytes 3932164
  41.6 56.9 %collective-permute-start.1 = (bf16[1280,1024]{1,0:T(8,128)(2,1)S(1)}, bf16[1280,1024]{1,0:T(8,128)(2,1)S(1)}, u32[]{:S(2)}, u32[]{:S(2)}) collective-permute-start(bf16[1280,1024]{1,0:T(8,128)(2,1)S(1)} %pad_maximum_fusion.1), channel_id=1, source_target_pairs={{0,12},{2,14},{4,0},{6,2},{8,4},{10,6},{12,8},{14,10},{1,13},{3,15... | collective-permute-start | bytes 7864328 | tf_op jit(solution)/shard_map/ppermute | solution.py:28
  43.2 58.8 %copy-start.17 = (s32[128]{0:T(128)S(1)}, s32[128]{0:T(128)}, u32[]{:S(2)}) copy-start(s32[128]{0:T(128)} %param.26) | copy-start | bytes 1540
  43.2 58.9 %copy-start.21 = (f32[1280]{0:T(1024)S(1)}, f32[1280]{0:T(1024)}, u32[]{:S(2)}) copy-start(f32[1280]{0:T(1024)} %param.19) | copy-start | bytes 15364
  43.2 58.9 %copy-start.22 = (f32[1280]{0:T(1024)S(1)}, f32[1280]{0:T(1024)}, u32[]{:S(2)}) copy-start(f32[1280]{0:T(1024)} %param.18) | copy-start | bytes 15364
  98.6 3.2 copy-start.3
  101.7 4.2 copy-start.16
  101.7 4.4 copy-start.15
  101.8 5.9 %copy-start.18 = (s32[8,2]{0,1:T(2,128)S(1)}, s32[8,2]{0,1:T(2,128)}, u32[]{:S(2)}) copy-start(s32[8,2]{0,1:T(2,128)} %param.25) | copy-start | bytes 196
  101.8 228.0 %collective-permute-start.2 = (bf16[2560,1024]{1,0:T(8,128)(2,1)}, bf16[2560,1024]{1,0:T(8,128)(2,1)}, u32[]{:S(2)}, u32[]{:S(2)}) collective-permute-start(bf16[2560,1024]{1,0:T(8,128)(2,1)} %pad_maximum_fusion), channel_id=1, source_target_pairs={{0,8},{2,10},{4,12},{6,14},{8,0},{10,2},{12,4},{14,6},{1,9},{3,11}... | collective-permute-start | bytes 15728648 | tf_op jit(solution)/shard_map/ppermute | solution.py:28
  103.0 44.1 %copy-start.13 = (f32[1280]{0:T(1024)S(1)}, f32[1280]{0:T(1024)}, u32[]{:S(2)}) copy-start(f32[1280]{0:T(1024)} %param.23) | copy-start | bytes 15364
  103.0 44.1 %copy-start.14 = (f32[1280]{0:T(1024)S(1)}, f32[1280]{0:T(1024)}, u32[]{:S(2)}) copy-start(f32[1280]{0:T(1024)} %param.22) | copy-start | bytes 15364
  105.9 42.8 %copy-start.8 = (bf16[640,1024]{1,0:T(8,128)(2,1)S(1)}, bf16[640,1024]{1,0:T(8,128)(2,1)}, u32[]{:S(2)}) copy-start(bf16[640,1024]{1,0:T(8,128)(2,1)} %copy-done.7) | copy-start | bytes 3932164
  153.3 181.8 %copy-start.6 = (bf16[640,1024]{1,0:T(8,128)(2,1)S(1)}, bf16[640,1024]{1,0:T(8,128)(2,1)}, u32[]{:S(2)}) copy-start(bf16[640,1024]{1,0:T(8,128)(2,1)} %param.24) | copy-start | bytes 3932164
  153.4 183.0 %copy-start.9 = (bf16[640,1024]{1,0:T(8,128)(2,1)S(1)}, bf16[640,1024]{1,0:T(8,128)(2,1)}, u32[]{:S(2)}) copy-start(bf16[640,1024]{1,0:T(8,128)(2,1)} %copy-done.7) | copy-start | bytes 3932164
  335.2 2.4 copy-start.4
  352.2 18.1 %all-to-all-start = ((bf16[8,4,1024]{2,1,0:T(4,128)(2,1)}), bf16[8,4,1024]{2,1,0:T(4,128)(2,1)S(1)}, u32[]{:S(2)}, u32[]{:S(2)}) async-start(bf16[8,4,1024]{2,1,0:T(4,128)(2,1)} %reshape.661), calls=%async_computation | async-start | bytes 131072 | tf_op jit(solution)/shard_map/all_to_all | solution.py:158
  358.9 31.1 %all-gather.3.cloned.1.call-start = ((), (), s32[]{:S(2)}) async-start(), calls=%async_computation.2 | async-start | bytes 1310720 | tf_op jit(solution)/shard_map/all_gather | solution.py:180
  363.8 6.5 %copy-start.12 = (bf16[128,1024]{1,0:T(8,128)(2,1)S(1)}, bf16[128,1024]{1,0:T(8,128)(2,1)}, u32[]{:S(2)}) copy-start(bf16[128,1024]{1,0:T(8,128)(2,1)} %param.30) | copy-start | bytes 786436
  363.8 8.0 %copy-start.2 = (s32[1024]{0:T(1024)S(1)}, s32[1024]{0:T(1024)}, u32[]{:S(2)}) copy-start(s32[1024]{0:T(1024)} %param.29) | copy-start | bytes 12292
  363.8 27.7 %copy-start.20 = (f32[4096]{0:T(1024)S(1)}, f32[4096]{0:T(1024)}, u32[]{:S(2)}) copy-start(f32[4096]{0:T(1024)} %param.31) | copy-start | bytes 49156
  371.3 61.5 %all-gather.5.cloned.1.call-start = ((), (), s32[]{:S(2)}) async-start(), calls=%async_computation.3 | async-start | bytes 1179648 | tf_op jit(solution)/shard_map/all_gather | solution.py:208
  421.7 14.6 %copy-start.11 = (bf16[128,4096]{1,0:T(8,128)(2,1)S(1)}, bf16[128,4096]{1,0:T(8,128)(2,1)}, u32[]{:S(2)}) copy-start(bf16[128,4096]{1,0:T(8,128)(2,1)} %all-gather.3.cloned.1.call-done) | copy-start | bytes 3145732
  432.8 9.5 %collective-permute-start.3 = (bf16[1024,4,128]{0,2,1:T(8,128)(2,1)}, bf16[1024,4,128]{0,2,1:T(8,128)(2,1)S(1)}, u32[]{:S(2)}, u32[]{:S(2)}) collective-permute-start(bf16[1024,4,128]{0,2,1:T(8,128)(2,1)} %all-gather.5.cloned.1.call-done), channel_id=1, source_target_pairs={{0,1},{1,0},{2,3},{3,2},{4,5},{5,4},{6,7},{7,6},{8,9},{9,8},{10,11... | collective-permute-start | bytes 3145736 | tf_op jit(solution)/shard_map/ppermute | solution.py:39
  436.3 6.0 %copy-start.19 = (bf16[1024,4,128]{0,2,1:T(8,128)(2,1)S(1)}, bf16[1024,4,128]{0,2,1:T(8,128)(2,1)}, u32[]{:S(2)}) copy-start(bf16[1024,4,128]{0,2,1:T(8,128)(2,1)} %all-gather.5.cloned.1.call-done) | copy-start | bytes 3145732
  444.4 2.2 copy-start.1
Sparse Core Ops, SparseCore 0:
  106.0 38.5 all-reduce.1
  371.4 18.5 all-gather.2
  396.2 36.5 all-gather.4
